TPU v7x, 512 devices: a whole 4x8x8 slice. The times are simulated.
512 devices in a mesh: ta: 32 (over y, x), pb: 16 (over z, core).
Axes of the slice: x: 4, y: 8, z: 8, core: 2. Of those that a mesh axis runs over, the one named last changes fastest.
Arguments:
- particles: float32 [2, 2097152], P(None, ('ta', 'pb')), may hold values from -6 to 6
- weights: bfloat16 [2097152], P(('ta', 'pb')), may hold values from 0.5 to 2
- cell_index: int32 [2097152], P(('ta', 'pb')), may hold values from 0 to 9215
- target_group: int32 [2097152, 1], P(('ta', 'pb')), may hold values from 0 to 31; in each aligned block of 4096 rows (0 to 4095, 4096 to 8191, ...) at most 256 rows name the same one
- target_slice: int32 [2097152], P(('ta', 'pb')), may hold values from 0 to 3
- laser_x: float32 [96], replicated, may hold values from 0.3 to 1.5
- laser_y: float32 [96], replicated, may hold values from 0.3 to 1.5
- mode_x: float32 [96], replicated, may hold values from 0.3 to 1.5
- mode_y: float32 [96], replicated, may hold values from 0.3 to 1.5
- along_coeff: float32 [96, 96], replicated, may hold values from 0.2 to 2
- across_coeff: float32 [96, 96], replicated, may hold values from 0.1 to 1
Outputs:
- arrivals: float32 [2, 4194304], P(None, ('ta', 'pb'))
- radiation: float32 [2, 128], P(None, 'ta')
Inputs may be any that keep to these rules, and one draw needn't show every extreme that they name: `target_group`: in the rows of one device at most 256 rows name the same group, and in every draw some group is named by exactly 256 rows of some device.
All inputs are finite; a program needn't handle non-finite values.
Results may differ from a plain program's by a relative error of at most 0.0009.
Values sent between devices are 32-bit elements; how exact they have to be, the bound alone decides.
No kernel may reach another device: no remote copies, remote signals or barrier semaphores. Data moves between devices by JAX's collectives and lax.ppermute only.
A program may use at most 64 MiB of HBM per device.

v0:
```python
import math
import jax
import jax.numpy as jnp
from jax import lax
from jax.sharding import PartitionSpec as P

SL_DEV = 4
PS_DEV = 1024
HARM = 48
PERIODS = 2
DISPERSION = 3.0
LASER_GAIN = 1.0
KICK_GAIN = 0.5
SLIP_GAIN = 0.05


def with_halo(x, sides, width):
    for axis, dim in sides:
        peers, length = (lax.axis_size(axis), x.shape[dim])
        up = [(i, (i + 1) % peers) for i in range(peers - 1)]
        down = [(j, i) for i, j in up]
        last = lax.slice_in_dim(x, length - width, length, axis=dim)
        leading = lax.slice_in_dim(x, 0, width, axis=dim)
        before = lax.ppermute(last, axis, up)
        after = lax.ppermute(leading, axis, down)
        x = jnp.concatenate([before, x, after], axis=dim)
    return x


def shifted(value, axis, steps):
    count = lax.axis_size(axis)
    leading, last = (max(0, -steps), min(count, count - steps))
    return lax.ppermute(value, axis, [(source, source + steps) for source in range(leading, last)])


def lookup(values_table, positions):
    matches = positions[None, :] == jnp.arange(values_table.shape[0], dtype=jnp.int32)[:, None]
    return jnp.sum(jnp.where(matches, values_table[:, None], 0.0), axis=0)


def arrival_slots(destination, groups):
    count = destination.shape[0]
    block_size = math.gcd(count, 512)
    turn_count = count // block_size
    onehot = (destination[:, None] == jnp.arange(groups, dtype=jnp.int32)[None, :]).astype(
        jnp.bfloat16
    )
    onehot = onehot.reshape(turn_count, block_size, groups)
    earlier = (jnp.arange(block_size)[:, None] > jnp.arange(block_size)[None, :]).astype(
        jnp.bfloat16
    )

    def count_step(counted, onehot_rows):
        before = (
            jnp.dot(earlier, onehot_rows, preferred_element_type=jnp.float32) + counted[None, :]
        )
        rows_f = onehot_rows.astype(jnp.float32)
        return (counted + jnp.sum(rows_f, axis=0), jnp.sum(before * rows_f, axis=1))

    _, arrival = lax.scan(count_step, jnp.zeros((groups,), jnp.float32), onehot)
    return arrival.reshape(count).astype(jnp.int32)


def deposit(arrived_weight, got_slice, got_cell, slice_count, grid_x, grid_y):
    slot_count = arrived_weight.shape[0]
    block_size = math.gcd(slot_count, 2048)
    turn_count = slot_count // block_size
    block_items = (
        arrived_weight.reshape(turn_count, block_size),
        got_slice.reshape(turn_count, block_size),
        got_cell.reshape(turn_count, block_size),
    )

    def deposit_step(running, items):
        block_weight, block_slice, block_cell = items
        on_slice = block_slice[None, :] == jnp.arange(slice_count, dtype=jnp.int32)[:, None]
        on_row = (block_cell // grid_y)[None, :] == jnp.arange(grid_x, dtype=jnp.int32)[:, None]
        left = jnp.where(
            on_slice[:, None, :] & on_row[None, :, :],
            block_weight[None, None, :],
            jnp.zeros((), jnp.bfloat16),
        )
        left = left.reshape(slice_count * grid_x, block_size)
        right = (
            (block_cell % grid_y)[:, None] == jnp.arange(grid_y, dtype=jnp.int32)[None, :]
        ).astype(jnp.bfloat16)
        return (running + jnp.dot(left, right, preferred_element_type=jnp.float32), None)

    running, _ = lax.scan(
        deposit_step, jnp.zeros((slice_count * grid_x, grid_y), jnp.float32), block_items
    )
    return running.reshape(slice_count, grid_x * grid_y)


def stencil(extended, sideways, coeff_long, coeff_cross, grid_y):
    centre = sideways[:, grid_y:-grid_y]
    along_diff = extended[2:] - extended[:-2]
    across = sideways[:, 2 * grid_y :] + sideways[:, : -2 * grid_y]
    column = jnp.arange(centre.shape[1], dtype=jnp.int32) % grid_y
    upper_y = jnp.where(column < grid_y - 1, jnp.pad(centre, ((0, 0), (0, 1)))[:, 1:], 0.0)
    lower_y = jnp.where(column > 0, jnp.pad(centre, ((0, 0), (1, 0)))[:, :-1], 0.0)
    return coeff_long[None, :] * along_diff + coeff_cross[None, :] * (
        4.0 * centre - across - upper_y - lower_y
    )


def body(
    particles,
    weights,
    cell_index,
    target_group,
    target_slice,
    laser_x,
    laser_y,
    mode_x,
    mode_y,
    along_coeff,
    across_coeff,
):
    groups = lax.axis_size("ta")
    splits = lax.axis_size("pb")
    grid_x = laser_x.shape[0]
    grid_y = laser_y.shape[0]
    cell_count = grid_x * grid_y
    per_device = particles.shape[1]
    capacity = 2 * per_device // groups
    slot_count = groups * capacity
    row_x = cell_index // grid_y
    row_y = cell_index % grid_y
    energy = particles[1] + LASER_GAIN * lookup(laser_x, row_x) * lookup(laser_y, row_y) * jnp.sin(
        particles[0]
    )
    phases = particles[0] + DISPERSION * energy
    destination = target_group[:, 0]
    position = destination * capacity + arrival_slots(destination, groups)
    send_float = (
        jnp.zeros((3, slot_count), jnp.float32)
        .at[:, position]
        .set(jnp.stack([phases, energy, weights.astype(jnp.float32)]))
    )
    send_index = (
        jnp.zeros((1, slot_count), jnp.int32)
        .at[0, position]
        .set(target_slice * cell_count + cell_index)
    )
    got_float, got_index = (
        lax.all_to_all(
            send_float.reshape(3, groups, capacity), "ta", split_axis=1, concat_axis=1, tiled=True
        ),
        lax.all_to_all(
            send_index.reshape(1, groups, capacity), "ta", split_axis=1, concat_axis=1, tiled=True
        ),
    )
    got_float = got_float.reshape(3, slot_count)
    combined = got_index.reshape(slot_count)
    arrived_weight = got_float[2]
    got_slice = combined // cell_count
    got_cell = combined % cell_count
    partial_value = deposit(
        arrived_weight.astype(jnp.bfloat16), got_slice, got_cell, SL_DEV, grid_x, grid_y
    )
    long_flat = along_coeff.reshape(cell_count)
    cross_flat = across_coeff.reshape(cell_count)
    summed = lax.psum(partial_value, "pb")
    extended = with_halo(summed, (("ta", 0),), 1)
    sideways = jnp.pad(extended[1:-1], ((0, 0), (grid_y, grid_y)))
    force_map = stencil(extended, sideways, long_flat, cross_flat, grid_y)
    kicked = got_float[1] + jnp.take(force_map.reshape(-1), combined)
    got_phase = got_float[0]
    profile = lookup(mode_x, got_cell // grid_y) * lookup(mode_y, got_cell % grid_y)
    weighted = arrived_weight * profile
    select = (got_slice[None, :] == jnp.arange(SL_DEV, dtype=jnp.int32)[:, None]).astype(
        jnp.float32
    )
    couple = 1.0 / math.sqrt(splits * PS_DEV)
    radiation = jnp.zeros((2, SL_DEV), jnp.float32)
    for period in range(PERIODS):
        harmonic_phase = HARM * got_phase
        cosine = jnp.cos(harmonic_phase)
        sine_part = jnp.sin(harmonic_phase)
        local_sums = jnp.stack(
            [
                jnp.sum(select * (weighted * cosine)[None, :], axis=1),
                jnp.sum(select * (-weighted * sine_part)[None, :], axis=1),
            ]
        )
        bunching = lax.psum(local_sums, "pb")
        radiation = radiation + couple * bunching
        real_here = jnp.sum(select * radiation[0][:, None], axis=0)
        imag_here = jnp.sum(select * radiation[1][:, None], axis=0)
        kicked = kicked + KICK_GAIN * profile * (real_here * cosine - imag_here * sine_part)
        got_phase = got_phase + SLIP_GAIN * kicked
        incoming = shifted(radiation[:, -1:], "ta", 1)
        radiation = jnp.concatenate([incoming, radiation[:, :-1]], axis=1)
    filled = arrived_weight > 0
    result = jnp.stack([jnp.where(filled, got_phase, 0.0), jnp.where(filled, kicked, 0.0)])
    return (result, radiation)


def solution(mesh):
    return jax.shard_map(
        body,
        mesh=mesh,
        in_specs=(
            P(None, ("ta", "pb")),
            P(("ta", "pb")),
            P(("ta", "pb")),
            P(("ta", "pb"), None),
            P(("ta", "pb")),
            P(),
            P(),
            P(),
            P(),
            P(),
            P(),
        ),
        out_specs=(P(None, ("ta", "pb")), P(None, "ta")),
        check_vma=False,
    )
```

profile of v0, /device:TPU:32, one launch (start us, length us, event | category | flops | bytes accessed | tf_op | source)
XLA Modules:
  0.0 320.8 jit_solution(3291533808186617567)
XLA Ops:
  7.3 0.5 broadcast.560
  7.8 1.4 reduce.17
  9.3 4.0 %while.26 = (s32[]{:T(128)}, f32[32]{0:T(128)S(1)}, f32[8,512]{1,0:T(8,128)S(1)}, bf16[8,512,32]{1,2,0:T(8,128)(2,1)S(1)}, s32[]{:T(128)}, /*index=5*/s32[]{:T(128)}) while((s32[]{:T(128)}, f32[32]{0:T(128)S(1)}, f32[8,512]{1,0:T(8,128)S(1)}, bf16[8,512,32]{1,2,0:T(8,128)(2,1)S(1)}, s32[]{:T(128)}, /*index=5*/s32[]{:T(128)}) %tuple.81), condition=%wide.region_3.4_spmd.clone, body=%wide.region_0.3_spmd.clone.sunk | while | flops 17399332 | bytes 106719 | solution.py:60
  9.3 0.1 convert_reduce_fusion.3
  9.4 0.3 fusion.48
  9.9 0.3 fusion.48
  10.3 0.1 convert_reduce_fusion.3
  10.4 0.3 fusion.48
  10.9 0.3 fusion.48
  11.4 0.3 fusion.48
  11.9 0.3 fusion.48
  12.4 0.3 fusion.48
  12.9 0.3 fusion.48
  13.4 0.1 and_reduce_fusion
  13.7 16.1 %scatter_custom_fusion.1 = s32[8192]{0:T(1024)} fusion(s32[4096]{0:T(1024)S(1)} %broadcast_select_fusion.2, s32[4096]{0:T(1024)S(1)} %get-tuple-element.186, s32[]{:T(128)} %constant.147.clone.1), kind=kCustom, calls=%fused_computation.109 | custom fusion | bytes 32772
  29.8 9.8 %all-to-all-start.1 = ((s32[1,32,256]{2,0,1:T(1,128)}), s32[1,32,256]{2,0,1:T(1,128)S(1)}, u32[]{:S(2)}, u32[]{:S(2)}) async-start(s32[1,32,256]{2,0,1:T(1,128)} %bitcast.8), calls=%async_computation.1 | async-start | bytes 65536 | tf_op jit(solution)/shard_map/all_to_all | solution.py:150
  39.7 0.5 select_reduce_fusion.2
  40.2 0.5 multiply_add_fusion.4
  40.8 0.6 copy.23
  41.4 12.8 %scatter_custom_fusion = f32[3,8192]{0,1:T(8,128)} fusion(s32[4096]{0:T(1024)S(1)} %bitcast.101, f32[4096,3]{1,0:T(8,128)S(1)} %copy.23, f32[]{:T(128)} %constant.145.clone.1), kind=kCustom, calls=%fused_computation.31 | custom fusion | bytes 98308 | tf_op jit(solution)/shard_map/scatter | solution.py:139
  54.2 3.5 %copy.24 = f32[3,32,256]{2,0,1:T(4,128)} copy(f32[3,32,256]{0,2,1:T(8,128)} %bitcast.82) | data formatting | bytes 196608 | tf_op jit(solution)/shard_map/reshape | solution.py:148
  57.9 9.8 %all-to-all-start = ((f32[3,32,256]{2,0,1:T(4,128)}), f32[3,32,256]{2,0,1:T(4,128)S(1)}, u32[]{:S(2)}, u32[]{:S(2)}) async-start(f32[3,32,256]{2,0,1:T(4,128)} %copy.24), calls=%async_computation | async-start | bytes 262144 | tf_op jit(solution)/shard_map/all_to_all | solution.py:147
  67.8 0.2 remainder_reduce_fusion
  68.1 0.1 compare_reduce_fusion
  68.4 1.0 select_reduce_fusion
  69.4 4.2 %all-to-all-done = f32[3,32,256]{2,0,1:T(4,128)S(1)} async-done(((f32[3,32,256]{2,0,1:T(4,128)}), f32[3,32,256]{2,0,1:T(4,128)S(1)}, u32[]{:S(2)}, u32[]{:S(2)}) %all-to-all-start) | async-done | bytes 98336 | tf_op jit(solution)/shard_map/all_to_all | solution.py:147
  73.7 0.1 negate_multiply_fusion
  73.8 0.1 fusion.32
  74.0 0.2 select_reduce_fusion.11
  74.2 30.3 %psum.22 = f32[2,4]{1,0:T(2,128)S(1)} all-reduce(f32[2,4]{1,0:T(2,128)S(1)} %pad_maximum_fusion.3), channel_id=1, replica_groups=mesh['ta'=32,'pb'=16] {'pb'}, use_global_device_ids=true, to_apply=%region_15.16 | all-reduce | flops 8 | bytes 64 | tf_op jit(solution)/shard_map/psum | solution.py:187
  104.6 8.0 %while.27 = (s32[]{:T(128)}, f32[384,96]{0,1:T(8,128)S(1)}, s32[4,2048]{1,0:T(4,128)S(1)}, s32[4,2048]{1,0:T(4,128)S(1)}, bf16[4,2048]{1,0:T(4,128)(2,1)S(1)}, /*index=5*/s32[]{:T(128)}, s32[]{:T(128)}) while((s32[]{:T(128)}, f32[384,96]{0,1:T(8,128)S(1)}, s32[4,2048]{1,0:T(4,128)S(1)}, s32[4,2048]{1,0:T(4,128)S(1)}, ...), condition=%wide.region_9.10_spmd.clone, body=%wide.region_8.9_spmd.clone.sunk | while | flops 153069568 | bytes 5517415 | solution.py:89
  104.8 0.5 broadcast_and_fusion.2
  105.4 0.2 bitcast_select_fusion.2
  105.6 1.0 convolution_add_fusion.3
  106.9 0.5 broadcast_and_fusion.2
  107.4 0.2 bitcast_select_fusion.2
  107.6 1.0 convolution_add_fusion.3
  108.9 0.5 broadcast_and_fusion.2
  109.4 0.2 bitcast_select_fusion.2
  109.6 1.0 convolution_add_fusion.3
  110.9 0.5 broadcast_and_fusion.2
  111.4 0.2 bitcast_select_fusion.2
  111.6 1.0 convolution_add_fusion.3
  112.7 0.1 copy.25
  112.8 0.8 reshape.556
  113.7 2.5 collective-permute-start.2
  116.2 101.6 %all-reduce.6.cloned.1.call-done = f32[4,9216]{1,0:T(4,128)} async-done(((f32[4,9216]{1,0:T(4,128)}), f32[4,9216]{1,0:T(4,128)}) %all-reduce.6.cloned.1.call-update) | async-done | bytes 147472 | tf_op jit(solution)/shard_map/psum | solution.py:164
  217.9 1.0 fusion.37
  218.9 3.4 %collective-permute-start.1 = (f32[1,9216]{1,0:T(1,128)S(1)}, f32[1,9216]{1,0:T(1,128)S(1)}, u32[]{:S(2)}, u32[]{:S(2)}) collective-permute-start(f32[1,9216]{1,0:T(1,128)S(1)} %get-tuple-element.177), channel_id=1, source_target_pairs={{0,16},{16,32},{32,48},{48,64},{64,80},{80,96},{96,112},{112,128},... | collective-permute-start | bytes 110600 | tf_op jit(solution)/shard_map/ppermute | solution.py:24
  222.3 6.0 %collective-permute-start = (f32[1,9216]{1,0:T(1,128)S(1)}, f32[1,9216]{1,0:T(1,128)S(1)}, u32[]{:S(2)}, u32[]{:S(2)}) collective-permute-start(f32[1,9216]{1,0:T(1,128)S(1)} %get-tuple-element.176), channel_id=1, source_target_pairs={{16,0},{32,16},{48,32},{64,48},{80,64},{96,80},{112,96},{128,112},... | collective-permute-start | bytes 110600 | tf_op jit(solution)/shard_map/ppermute | solution.py:25
  228.3 0.2 select_reduce_fusion.9
  228.5 1.2 collective-permute-done
  229.7 2.0 fusion.19
  231.8 45.5 %gather_fusion = f32[8192]{0:T(1024)S(1)} fusion(f32[36864]{0:T(1024)S(1)} %bitcast.81, s32[8192]{0:T(1024)S(1)} %broadcast_clamp_fusion), kind=kCustom, calls=%fused_computation | custom fusion | bytes 98304 | tf_op jit(solution)/shard_map/jit(_take)/gather | solution.py:168
  277.3 0.3 sine_multiply_fusion
  277.6 0.1 cosine_multiply_fusion
  277.7 0.2 select_reduce_fusion.7
  278.0 23.5 %psum.23 = f32[2,4]{1,0:T(2,128)S(1)} all-reduce(f32[2,4]{1,0:T(2,128)S(1)} %pad_maximum_fusion.4), channel_id=1, replica_groups=mesh['ta'=32,'pb'=16] {'pb'}, use_global_device_ids=true, to_apply=%region_20.21 | all-reduce | flops 8 | bytes 64 | tf_op jit(solution)/shard_map/psum | solution.py:187
  301.7 0.2 select_reduce_fusion.5
  301.9 2.2 add_select_fusion.8
  304.3 1.9 collective-permute-start.3
  306.2 0.7 pad_maximum_fusion.2
  306.9 6.5 %collective-permute-done.3 = f32[2,1]{1,0:T(2,128)S(1)} collective-permute-done((f32[2,1]{1,0:T(2,128)S(1)}, f32[2,1]{1,0:T(2,128)S(1)}, u32[]{:S(2)}, u32[]{:S(2)}) %collective-permute-start.3) | collective-permute-done | bytes 40 | tf_op jit(solution)/shard_map/ppermute | solution.py:33
  313.4 0.6 pad_maximum_fusion.5
  (111 shorter events, 3.6 us)
Async XLA Ops:
  7.2 6.2 %copy-start.12 = (s32[2]{0:T(128)S(1)}, s32[2]{0:T(128)}, u32[]{:S(2)}) copy-start(s32[2]{0:T(128)} %constant.174) | copy-start | bytes 28
  7.2 6.3 %copy-start.11 = (s32[2]{0:T(128)S(1)}, s32[2]{0:T(128)}, u32[]{:S(2)}) copy-start(s32[2]{0:T(128)} %constant.171) | copy-start | bytes 28
  7.2 6.1 %copy-start = (s32[4096,1]{0,1:T(1,128)S(1)}, s32[4096,1]{0,1:T(1,128)}, u32[]{:S(2)}) copy-start(s32[4096,1]{0,1:T(1,128)} %param.18) | copy-start | bytes 49156
  7.2 6.4 %copy-start.4 = (s32[4096]{0:T(1024)S(1)}, s32[4096]{0:T(1024)}, u32[]{:S(2)}) copy-start(s32[4096]{0:T(1024)} %param.17) | copy-start | bytes 49156
  7.2 6.4 %copy-start.5 = (s32[4096]{0:T(1024)S(1)}, s32[4096]{0:T(1024)}, u32[]{:S(2)}) copy-start(s32[4096]{0:T(1024)} %param.19) | copy-start | bytes 49156
  7.2 32.4 %copy-start.6 = (bf16[4096]{0:T(1024)(128)(2,1)S(1)}, bf16[4096]{0:T(1024)(128)(2,1)}, u32[]{:S(2)}) copy-start(bf16[4096]{0:T(1024)(128)(2,1)} %param.16) | copy-start | bytes 24580
  7.2 32.4 %copy-start.7 = (f32[96]{0:T(128)S(1)}, f32[96]{0:T(128)}, u32[]{:S(2)}) copy-start(f32[96]{0:T(128)} %param.21) | copy-start | bytes 1156
  7.2 32.4 %copy-start.8 = (f32[96]{0:T(128)S(1)}, f32[96]{0:T(128)}, u32[]{:S(2)}) copy-start(f32[96]{0:T(128)} %param.20) | copy-start | bytes 1156
  7.3 33.0 %copy-start.3 = (f32[2,4096]{1,0:T(2,128)S(1)}, f32[2,4096]{1,0:T(2,128)}, u32[]{:S(2)}) copy-start(f32[2,4096]{1,0:T(2,128)} %param.15) | copy-start | bytes 98308
  29.8 28.1 %all-to-all-start.1 = ((s32[1,32,256]{2,0,1:T(1,128)}), s32[1,32,256]{2,0,1:T(1,128)S(1)}, u32[]{:S(2)}, u32[]{:S(2)}) async-start(s32[1,32,256]{2,0,1:T(1,128)} %bitcast.8), calls=%async_computation.1 | async-start | bytes 65536 | tf_op jit(solution)/shard_map/all_to_all | solution.py:150
  54.2 3.5 %copy-start.1 = (f32[96,96]{1,0:T(8,128)S(1)}, f32[96,96]{1,0:T(8,128)}, u32[]{:S(2)}) copy-start(f32[96,96]{1,0:T(8,128)} %param.25) | copy-start | bytes 110596
  54.2 3.6 %copy-start.2 = (f32[96,96]{1,0:T(8,128)S(1)}, f32[96,96]{1,0:T(8,128)}, u32[]{:S(2)}) copy-start(f32[96,96]{1,0:T(8,128)} %param.24) | copy-start | bytes 110596
  54.2 14.2 %copy-start.9 = (f32[96]{0:T(128)S(1)}, f32[96]{0:T(128)}, u32[]{:S(2)}) copy-start(f32[96]{0:T(128)} %param.23) | copy-start | bytes 1156
  54.2 14.2 %copy-start.10 = (f32[96]{0:T(128)S(1)}, f32[96]{0:T(128)}, u32[]{:S(2)}) copy-start(f32[96]{0:T(128)} %param.22) | copy-start | bytes 1156
  57.9 15.7 %all-to-all-start = ((f32[3,32,256]{2,0,1:T(4,128)}), f32[3,32,256]{2,0,1:T(4,128)S(1)}, u32[]{:S(2)}, u32[]{:S(2)}) async-start(f32[3,32,256]{2,0,1:T(4,128)} %copy.24), calls=%async_computation | async-start | bytes 262144 | tf_op jit(solution)/shard_map/all_to_all | solution.py:147
  67.7 150.2 %all-reduce.6.cloned.1.call-start = ((), (), s32[]{:S(2)}) async-start(), calls=%async_computation.2 | async-start | bytes 294912 | tf_op jit(solution)/shard_map/psum | solution.py:164
  113.7 187.8 %collective-permute-start.2 = (f32[2,1]{1,0:T(2,128)S(1)}, f32[2,1]{1,0:T(2,128)S(1)}, u32[]{:S(2)}, u32[]{:S(2)}) collective-permute-start(f32[2,1]{1,0:T(2,128)S(1)} %slice.85), channel_id=1, source_target_pairs={{0,16},{16,32},{32,48},{48,64},{64,80},{80,96},{96,112},{112,128},... | collective-permute-start | bytes 32 | tf_op jit(solution)/shard_map/ppermute | solution.py:33
  218.9 9.6 %collective-permute-start.1 = (f32[1,9216]{1,0:T(1,128)S(1)}, f32[1,9216]{1,0:T(1,128)S(1)}, u32[]{:S(2)}, u32[]{:S(2)}) collective-permute-start(f32[1,9216]{1,0:T(1,128)S(1)} %get-tuple-element.177), channel_id=1, source_target_pairs={{0,16},{16,32},{32,48},{48,64},{64,80},{80,96},{96,112},{112,128},... | collective-permute-start | bytes 110600 | tf_op jit(solution)/shard_map/ppermute | solution.py:24
  222.3 7.4 %collective-permute-start = (f32[1,9216]{1,0:T(1,128)S(1)}, f32[1,9216]{1,0:T(1,128)S(1)}, u32[]{:S(2)}, u32[]{:S(2)}) collective-permute-start(f32[1,9216]{1,0:T(1,128)S(1)} %get-tuple-element.176), channel_id=1, source_target_pairs={{16,0},{32,16},{48,32},{64,48},{80,64},{96,80},{112,96},{128,112},... | collective-permute-start | bytes 110600 | tf_op jit(solution)/shard_map/ppermute | solution.py:25
  304.3 9.1 %collective-permute-start.3 = (f32[2,1]{1,0:T(2,128)S(1)}, f32[2,1]{1,0:T(2,128)S(1)}, u32[]{:S(2)}, u32[]{:S(2)}) collective-permute-start(f32[2,1]{1,0:T(2,128)S(1)} %slice.89), channel_id=1, source_target_pairs={{0,16},{16,32},{32,48},{48,64},{64,80},{80,96},{96,112},{112,128},... | collective-permute-start | bytes 32 | tf_op jit(solution)/shard_map/ppermute | solution.py:33
Sparse Core Ops, SparseCore 0:
  113.8 104.0 all-reduce.5
where the time goes:
time: 321 us
  waiting for transfers between devices  114 us (36%)
  local copies, waits for them, and re-layouts  82.4 us (26%)
  blocking collectives  53.8 us (17%)
  starting transfers between devices  33.4 us (10%)
  other arithmetic  16.3 us (5%)
  between operations  14.6 us (5%)
  matrix products  6.37 us (2%)
    psum x1, waiting for transfers between devices, body(): summed = lax.psum(partial_value, 'pb')  102 us
    psum x2, blocking collectives, body(): bunching = lax.psum(local_sums, 'pb')  53.8 us
    gather x1, local copies, waits for them, and re-layouts, body(): kicked = got_float[1] + jnp.take(force_map.reshape(-1), combined)  45.5 us
    unnamed x30, local copies, waits for them, and re-layouts  16.7 us
    scatter x1, local copies, waits for them, and re-layouts, body(): send_float = jnp.zeros((3, slot_count), jnp.float32).at[:, position].set(...  12.8 us
    all_to_all x1, starting transfers between devices, body(): lax.all_to_all(send_index.reshape(1, groups, capacity), 'ta', split_axis=...  9.83 us
    all_to_all x1, starting transfers between devices, body(): lax.all_to_all(send_float.reshape(3, groups, capacity), 'ta', split_axis=...  9.79 us
    ppermute x2, waiting for transfers between devices, shifted(): lax.ppermute(value, axis, [(source, source + steps) for source in range(l...  6.48 us
  transfers between devices with their start and end apart: 7, of which 4 were waited for; matrix products, arithmetic and copies ran while one was open for 22% of the time, Pallas kernels for 0%

commit v1 on v0

--- a/solution.py
+++ b/solution.py
@@ -12,6 +12,11 @@
 LASER_GAIN = 1.0
 KICK_GAIN = 0.5
 SLIP_GAIN = 0.05
+
+
+def add_all(x, axis):
+    parts = lax.all_gather(x, axis)
+    return jnp.sum(parts, axis=0)
 
 
 def with_halo(x, sides, width):
@@ -184,7 +189,7 @@
                 jnp.sum(select * (-weighted * sine_part)[None, :], axis=1),
             ]
         )
-        bunching = lax.psum(local_sums, "pb")
+        bunching = add_all(local_sums, "pb")
         radiation = radiation + couple * bunching
         real_here = jnp.sum(select * radiation[0][:, None], axis=0)
         imag_here = jnp.sum(select * radiation[1][:, None], axis=0)

time: 321 us -> 305 us (0.950)
  blocking collectives: 53.8 us -> 38 us
    psum x2 -> x0, blocking collectives: 53.8 us -> none  [body(): bunching = lax.psum(local_sums, 'pb')]
    all_gather x0 -> x2, blocking collectives: none -> 38 us  [add_all(): parts = lax.all_gather(x, axis)]
  transfers between devices with their start and end apart: 7 -> 7, of which waited for: 4 -> 4; matrix products, arithmetic and copies ran while one was open for 22% -> 23% of each run, Pallas kernels for 0% -> 0%
where the time goes in v1:
time: 305 us; the launch traced here: 304 us
  waiting for transfers between devices  113 us (37%)
  local copies, waits for them, and re-layouts  82.4 us (27%)
  blocking collectives  38 us (12%)
  starting transfers between devices  33.4 us (11%)
  other arithmetic  16.3 us (5%)
  between operations  14.6 us (5%)
  matrix products  6.37 us (2%)
    psum x1, waiting for transfers between devices, body(): summed = lax.psum(partial_value, 'pb')  101 us
    gather x1, local copies, waits for them, and re-layouts, body(): kicked = got_float[1] + jnp.take(force_map.reshape(-1), combined)  45.5 us
    all_gather x2, blocking collectives, add_all(): parts = lax.all_gather(x, axis)  38 us
    unnamed x30, local copies, waits for them, and re-layouts  16.7 us
    scatter x1, local copies, waits for them, and re-layouts, body(): send_float = jnp.zeros((3, slot_count), jnp.float32).at[:, position].set(...  12.8 us
    all_to_all x1, starting transfers between devices, body(): lax.all_to_all(send_index.reshape(1, groups, capacity), 'ta', split_axis=...  9.83 us
    all_to_all x1, starting transfers between devices, body(): lax.all_to_all(send_float.reshape(3, groups, capacity), 'ta', split_axis=...  9.79 us
    ppermute x2, waiting for transfers between devices, shifted(): lax.ppermute(value, axis, [(source, source + steps) for source in range(l...  6.48 us
  transfers between devices with their start and end apart: 7, of which 4 were waited for; matrix products, arithmetic and copies ran while one was open for 23% of the time, Pallas kernels for 0%

profile of v1, /device:TPU:32, one launch (start us, length us, event | category | flops | bytes accessed | tf_op | source)
XLA Modules:
  0.0 304.2 jit_solution(13047001155948594587)
XLA Ops:
  7.3 0.5 broadcast.560
  7.8 1.4 reduce.19
  9.3 4.0 %while.26 = (s32[]{:T(128)}, f32[32]{0:T(128)S(1)}, f32[8,512]{1,0:T(8,128)S(1)}, bf16[8,512,32]{1,2,0:T(8,128)(2,1)S(1)}, s32[]{:T(128)}, /*index=5*/s32[]{:T(128)}) while((s32[]{:T(128)}, f32[32]{0:T(128)S(1)}, f32[8,512]{1,0:T(8,128)S(1)}, bf16[8,512,32]{1,2,0:T(8,128)(2,1)S(1)}, s32[]{:T(128)}, /*index=5*/s32[]{:T(128)}) %tuple.81), condition=%wide.region_3.4_spmd.clone, body=%wide.region_0.3_spmd.clone.sunk | while | flops 17399332 | bytes 106719 | solution.py:65
  9.3 0.1 convert_reduce_fusion.3
  9.4 0.3 fusion.48
  9.9 0.3 fusion.48
  10.3 0.1 convert_reduce_fusion.3
  10.4 0.3 fusion.48
  10.9 0.3 fusion.48
  11.4 0.3 fusion.48
  11.9 0.3 fusion.48
  12.4 0.3 fusion.48
  12.9 0.3 fusion.48
  13.4 0.1 and_reduce_fusion
  13.7 16.1 %scatter_custom_fusion.1 = s32[8192]{0:T(1024)} fusion(s32[4096]{0:T(1024)S(1)} %broadcast_select_fusion.2, s32[4096]{0:T(1024)S(1)} %get-tuple-element.186, s32[]{:T(128)} %constant.147.clone.1), kind=kCustom, calls=%fused_computation.109 | custom fusion | bytes 32772
  29.8 9.8 %all-to-all-start.1 = ((s32[1,32,256]{2,0,1:T(1,128)}), s32[1,32,256]{2,0,1:T(1,128)S(1)}, u32[]{:S(2)}, u32[]{:S(2)}) async-start(s32[1,32,256]{2,0,1:T(1,128)} %bitcast.8), calls=%async_computation.1 | async-start | bytes 65536 | tf_op jit(solution)/shard_map/all_to_all | solution.py:155
  39.7 0.5 select_reduce_fusion.2
  40.2 0.5 multiply_add_fusion.4
  40.8 0.6 copy.23
  41.4 12.8 %scatter_custom_fusion = f32[3,8192]{0,1:T(8,128)} fusion(s32[4096]{0:T(1024)S(1)} %bitcast.105, f32[4096,3]{1,0:T(8,128)S(1)} %copy.23, f32[]{:T(128)} %constant.145.clone.1), kind=kCustom, calls=%fused_computation.31 | custom fusion | bytes 98308 | tf_op jit(solution)/shard_map/scatter | solution.py:144
  54.2 3.5 %copy.24 = f32[3,32,256]{2,0,1:T(4,128)} copy(f32[3,32,256]{0,2,1:T(8,128)} %bitcast.86) | data formatting | bytes 196608 | tf_op jit(solution)/shard_map/reshape | solution.py:153
  57.9 9.8 %all-to-all-start = ((f32[3,32,256]{2,0,1:T(4,128)}), f32[3,32,256]{2,0,1:T(4,128)S(1)}, u32[]{:S(2)}, u32[]{:S(2)}) async-start(f32[3,32,256]{2,0,1:T(4,128)} %copy.24), calls=%async_computation | async-start | bytes 262144 | tf_op jit(solution)/shard_map/all_to_all | solution.py:152
  67.8 0.2 remainder_reduce_fusion
  68.1 0.1 compare_reduce_fusion
  68.4 1.0 select_reduce_fusion
  69.4 4.2 %all-to-all-done = f32[3,32,256]{2,0,1:T(4,128)S(1)} async-done(((f32[3,32,256]{2,0,1:T(4,128)}), f32[3,32,256]{2,0,1:T(4,128)S(1)}, u32[]{:S(2)}, u32[]{:S(2)}) %all-to-all-start) | async-done | bytes 98336 | tf_op jit(solution)/shard_map/all_to_all | solution.py:152
  73.7 0.1 negate_multiply_fusion
  73.8 0.1 fusion.32
  74.0 0.2 select_reduce_fusion.11
  74.2 23.2 %all-gather.2 = f32[16,2,4]{2,1,0:T(2,128)S(1)} all-gather(f32[1,2,4]{2,1,0:T(2,128)S(1)} %maximum_bitcast_fusion.1), channel_id=2, replica_groups=mesh['ta'=32,'pb'=16] {'pb'}, dimensions={0}, use_global_device_ids=true | all-gather | bytes 544 | tf_op jit(solution)/shard_map/all_gather | solution.py:18
  97.6 8.0 %while.27 = (s32[]{:T(128)}, f32[384,96]{0,1:T(8,128)S(1)}, s32[4,2048]{1,0:T(4,128)S(1)}, s32[4,2048]{1,0:T(4,128)S(1)}, bf16[4,2048]{1,0:T(4,128)(2,1)S(1)}, /*index=5*/s32[]{:T(128)}, s32[]{:T(128)}) while((s32[]{:T(128)}, f32[384,96]{0,1:T(8,128)S(1)}, s32[4,2048]{1,0:T(4,128)S(1)}, s32[4,2048]{1,0:T(4,128)S(1)}, ...), condition=%wide.region_9.10_spmd.clone, body=%wide.region_8.9_spmd.clone.sunk | while | flops 153069568 | bytes 5517415 | solution.py:94
  97.8 0.5 broadcast_and_fusion.2
  98.3 0.2 bitcast_select_fusion.2
  98.5 1.0 convolution_add_fusion.3
  99.8 0.5 broadcast_and_fusion.2
  100.3 0.2 bitcast_select_fusion.2
  100.5 1.0 convolution_add_fusion.3
  101.8 0.5 broadcast_and_fusion.2
  102.3 0.2 bitcast_select_fusion.2
  102.5 1.0 convolution_add_fusion.3
  103.8 0.5 broadcast_and_fusion.2
  104.3 0.2 bitcast_select_fusion.2
  104.5 1.0 convolution_add_fusion.3
  105.6 0.1 copy.25
  105.7 0.8 reshape.556
  106.7 2.5 collective-permute-start.2
  109.2 100.7 %all-reduce.6.cloned.1.call-done = f32[4,9216]{1,0:T(4,128)} async-done(((f32[4,9216]{1,0:T(4,128)}), f32[4,9216]{1,0:T(4,128)}) %all-reduce.6.cloned.1.call-update) | async-done | bytes 147472 | tf_op jit(solution)/shard_map/psum | solution.py:169
  209.9 1.0 fusion.37
  211.0 3.4 %collective-permute-start.1 = (f32[1,9216]{1,0:T(1,128)S(1)}, f32[1,9216]{1,0:T(1,128)S(1)}, u32[]{:S(2)}, u32[]{:S(2)}) collective-permute-start(f32[1,9216]{1,0:T(1,128)S(1)} %get-tuple-element.177), channel_id=1, source_target_pairs={{0,16},{16,32},{32,48},{48,64},{64,80},{80,96},{96,112},{112,128},... | collective-permute-start | bytes 110600 | tf_op jit(solution)/shard_map/ppermute | solution.py:29
  214.4 6.0 %collective-permute-start = (f32[1,9216]{1,0:T(1,128)S(1)}, f32[1,9216]{1,0:T(1,128)S(1)}, u32[]{:S(2)}, u32[]{:S(2)}) collective-permute-start(f32[1,9216]{1,0:T(1,128)S(1)} %get-tuple-element.176), channel_id=1, source_target_pairs={{16,0},{32,16},{48,32},{64,48},{80,64},{96,80},{112,96},{128,112},... | collective-permute-start | bytes 110600 | tf_op jit(solution)/shard_map/ppermute | solution.py:30
  220.4 0.2 select_reduce_fusion.9
  220.6 1.2 collective-permute-done
  221.8 2.0 fusion.19
  223.8 45.5 %gather_fusion = f32[8192]{0:T(1024)S(1)} fusion(f32[36864]{0:T(1024)S(1)} %bitcast.85, s32[8192]{0:T(1024)S(1)} %broadcast_clamp_fusion), kind=kCustom, calls=%fused_computation | custom fusion | bytes 98304 | tf_op jit(solution)/shard_map/jit(_take)/gather | solution.py:173
  269.4 0.3 sine_multiply_fusion
  269.7 0.1 cosine_multiply_fusion
  269.8 0.2 select_reduce_fusion.7
  270.0 14.8 %all-gather.3 = f32[16,2,4]{2,1,0:T(2,128)S(1)} all-gather(f32[1,2,4]{2,1,0:T(2,128)S(1)} %maximum_bitcast_fusion.2), channel_id=3, replica_groups=mesh['ta'=32,'pb'=16] {'pb'}, dimensions={0}, use_global_device_ids=true | all-gather | bytes 544 | tf_op jit(solution)/shard_map/all_gather | solution.py:18
  285.0 0.2 select_reduce_fusion.5
  285.3 2.2 add_select_fusion.8
  287.6 1.9 collective-permute-start.3
  289.5 0.7 pad_maximum_fusion.2
  290.2 6.5 %collective-permute-done.3 = f32[2,1]{1,0:T(2,128)S(1)} collective-permute-done((f32[2,1]{1,0:T(2,128)S(1)}, f32[2,1]{1,0:T(2,128)S(1)}, u32[]{:S(2)}, u32[]{:S(2)}) %collective-permute-start.3) | collective-permute-done | bytes 40 | tf_op jit(solution)/shard_map/ppermute | solution.py:38
  296.7 0.6 pad_maximum_fusion.3
  (113 shorter events, 3.7 us)
Async XLA Ops:
  7.2 6.2 %copy-start.12 = (s32[2]{0:T(128)S(1)}, s32[2]{0:T(128)}, u32[]{:S(2)}) copy-start(s32[2]{0:T(128)} %constant.174) | copy-start | bytes 28
  7.2 6.3 %copy-start.11 = (s32[2]{0:T(128)S(1)}, s32[2]{0:T(128)}, u32[]{:S(2)}) copy-start(s32[2]{0:T(128)} %constant.171) | copy-start | bytes 28
  7.2 6.1 %copy-start = (s32[4096,1]{0,1:T(1,128)S(1)}, s32[4096,1]{0,1:T(1,128)}, u32[]{:S(2)}) copy-start(s32[4096,1]{0,1:T(1,128)} %param.18) | copy-start | bytes 49156
  7.2 6.4 %copy-start.4 = (s32[4096]{0:T(1024)S(1)}, s32[4096]{0:T(1024)}, u32[]{:S(2)}) copy-start(s32[4096]{0:T(1024)} %param.17) | copy-start | bytes 49156
  7.2 6.4 %copy-start.5 = (s32[4096]{0:T(1024)S(1)}, s32[4096]{0:T(1024)}, u32[]{:S(2)}) copy-start(s32[4096]{0:T(1024)} %param.19) | copy-start | bytes 49156
  7.2 32.4 %copy-start.6 = (bf16[4096]{0:T(1024)(128)(2,1)S(1)}, bf16[4096]{0:T(1024)(128)(2,1)}, u32[]{:S(2)}) copy-start(bf16[4096]{0:T(1024)(128)(2,1)} %param.16) | copy-start | bytes 24580
  7.2 32.4 %copy-start.7 = (f32[96]{0:T(128)S(1)}, f32[96]{0:T(128)}, u32[]{:S(2)}) copy-start(f32[96]{0:T(128)} %param.21) | copy-start | bytes 1156
  7.2 32.4 %copy-start.8 = (f32[96]{0:T(128)S(1)}, f32[96]{0:T(128)}, u32[]{:S(2)}) copy-start(f32[96]{0:T(128)} %param.20) | copy-start | bytes 1156
  7.3 33.0 %copy-start.3 = (f32[2,4096]{1,0:T(2,128)S(1)}, f32[2,4096]{1,0:T(2,128)}, u32[]{:S(2)}) copy-start(f32[2,4096]{1,0:T(2,128)} %param.15) | copy-start | bytes 98308
  29.8 28.1 %all-to-all-start.1 = ((s32[1,32,256]{2,0,1:T(1,128)}), s32[1,32,256]{2,0,1:T(1,128)S(1)}, u32[]{:S(2)}, u32[]{:S(2)}) async-start(s32[1,32,256]{2,0,1:T(1,128)} %bitcast.8), calls=%async_computation.1 | async-start | bytes 65536 | tf_op jit(solution)/shard_map/all_to_all | solution.py:155
  54.2 3.5 %copy-start.1 = (f32[96,96]{1,0:T(8,128)S(1)}, f32[96,96]{1,0:T(8,128)}, u32[]{:S(2)}) copy-start(f32[96,96]{1,0:T(8,128)} %param.25) | copy-start | bytes 110596
  54.2 3.6 %copy-start.2 = (f32[96,96]{1,0:T(8,128)S(1)}, f32[96,96]{1,0:T(8,128)}, u32[]{:S(2)}) copy-start(f32[96,96]{1,0:T(8,128)} %param.24) | copy-start | bytes 110596
  54.2 14.2 %copy-start.9 = (f32[96]{0:T(128)S(1)}, f32[96]{0:T(128)}, u32[]{:S(2)}) copy-start(f32[96]{0:T(128)} %param.23) | copy-start | bytes 1156
  54.2 14.2 %copy-start.10 = (f32[96]{0:T(128)S(1)}, f32[96]{0:T(128)}, u32[]{:S(2)}) copy-start(f32[96]{0:T(128)} %param.22) | copy-start | bytes 1156
  57.9 15.7 %all-to-all-start = ((f32[3,32,256]{2,0,1:T(4,128)}), f32[3,32,256]{2,0,1:T(4,128)S(1)}, u32[]{:S(2)}, u32[]{:S(2)}) async-start(f32[3,32,256]{2,0,1:T(4,128)} %copy.24), calls=%async_computation | async-start | bytes 262144 | tf_op jit(solution)/shard_map/all_to_all | solution.py:152
  67.7 142.2 %all-reduce.6.cloned.1.call-start = ((), (), s32[]{:S(2)}) async-start(), calls=%async_computation.2 | async-start | bytes 294912 | tf_op jit(solution)/shard_map/psum | solution.py:169
  106.7 178.2 %collective-permute-start.2 = (f32[2,1]{1,0:T(2,128)S(1)}, f32[2,1]{1,0:T(2,128)S(1)}, u32[]{:S(2)}, u32[]{:S(2)}) collective-permute-start(f32[2,1]{1,0:T(2,128)S(1)} %slice.85), channel_id=1, source_target_pairs={{0,16},{16,32},{32,48},{48,64},{64,80},{80,96},{96,112},{112,128},... | collective-permute-start | bytes 32 | tf_op jit(solution)/shard_map/ppermute | solution.py:38
  211.0 9.6 %collective-permute-start.1 = (f32[1,9216]{1,0:T(1,128)S(1)}, f32[1,9216]{1,0:T(1,128)S(1)}, u32[]{:S(2)}, u32[]{:S(2)}) collective-permute-start(f32[1,9216]{1,0:T(1,128)S(1)} %get-tuple-element.177), channel_id=1, source_target_pairs={{0,16},{16,32},{32,48},{48,64},{64,80},{80,96},{96,112},{112,128},... | collective-permute-start | bytes 110600 | tf_op jit(solution)/shard_map/ppermute | solution.py:29
  214.4 7.4 %collective-permute-start = (f32[1,9216]{1,0:T(1,128)S(1)}, f32[1,9216]{1,0:T(1,128)S(1)}, u32[]{:S(2)}, u32[]{:S(2)}) collective-permute-start(f32[1,9216]{1,0:T(1,128)S(1)} %get-tuple-element.176), channel_id=1, source_target_pairs={{16,0},{32,16},{48,32},{64,48},{80,64},{96,80},{112,96},{128,112},... | collective-permute-start | bytes 110600 | tf_op jit(solution)/shard_map/ppermute | solution.py:30
  287.6 9.1 %collective-permute-start.3 = (f32[2,1]{1,0:T(2,128)S(1)}, f32[2,1]{1,0:T(2,128)S(1)}, u32[]{:S(2)}, u32[]{:S(2)}) collective-permute-start(f32[2,1]{1,0:T(2,128)S(1)} %slice.89), channel_id=1, source_target_pairs={{0,16},{16,32},{32,48},{48,64},{64,80},{80,96},{96,112},{112,128},... | collective-permute-start | bytes 32 | tf_op jit(solution)/shard_map/ppermute | solution.py:38
Sparse Core Ops, SparseCore 0:
  106.7 103.1 all-reduce.5
